TPU v7x, 512 devices: a whole 4x8x8 slice. The times are simulated.
512 devices in a mesh: pool: 64 (over x, z, core), mp: 8 (over y).
Axes of the slice: x: 4, y: 8, z: 8, core: 2. Of those that a mesh axis runs over, the one named last changes fastest.
Arguments:
- residual_in: bfloat16 [16384, 2048], P('pool', 'mp'), may hold values from -6 to 6
- mlp_branch: bfloat16 [16384, 2048], P('pool'), may hold values from -6 to 6
- norm_gain: float32 [2048], replicated, may hold values from 0.5 to 1.5
- norm_bias: float32 [2048], replicated, may hold values from -3 to 3
- w_qkv: bfloat16 [2048, 3, 2048], P('pool', None, 'mp'), may hold values from -0.125 to 0.125
- qkv_bias: float32 [3, 2048], P(None, 'mp'), may hold values from -3 to 3
- cache_pool: bfloat16 [3072, 2, 32, 2048], P('pool', None, None, 'mp'), as said below
- w_dense: bfloat16 [2048, 2048], P('mp', 'pool'), may hold values from -0.125 to 0.125
- dense_bias: float32 [2048], replicated, may hold values from -3 to 3
- next_gain: float32 [2048], replicated, may hold values from 0.5 to 1.5
- next_bias: float32 [2048], replicated, may hold values from -3 to 3
- w_next: bfloat16 [2048, 3, 2048], P('pool', None, 'mp'), may hold values from -0.125 to 0.125
- next_qkv_bias: float32 [3, 2048], P(None, 'mp'), may hold values from -3 to 3
- token_request: int32 [16384], P('pool'), may hold values from 0 to 255, as said below
- cache_len: int32 [256], P('pool'), may hold values from 0 to 1024, as said below
- block_table: int32 [256, 32], P('pool'), may hold values from 0 to 3071, as said below
Outputs:
- hidden_out: bfloat16 [16384, 2048], P('pool', 'mp')
- next_qkv: bfloat16 [16384, 3, 2048], P('pool', None, 'mp')
Inputs may be any that keep to these rules, and one draw needn't show every extreme that they name: `token_request`: the 256 tokens of index i of pool belong to the requests i * 4 to (i+1) * 4 - 1, each request's tokens in one run, in increasing order, each request with at least one token. `cache_len`: 0 for a fresh prompt; some request has exactly 1024. `block_table`: block b is held by index b // 48 of pool; a block may appear in several lists; entries at or past a request's cached blocks are padding. Of the 128 entries of the requests of one index of pool, exactly 2 name blocks held by each index of pool. `cache_pool`: cached keys and values.
All inputs are finite; a program needn't handle non-finite values.
Results may differ from a plain program's by a relative error of at most 0.015.
Values may be sent and summed in bfloat16 or wider, within the bound.
No kernel may reach another device: no remote copies, remote signals or barrier semaphores. Data moves between devices by JAX's collectives and lax.ppermute only.
A program may use at most 128 MiB of HBM per device.

v0:
```python
import jax
import jax.numpy as jnp
from jax import lax
from jax.sharding import PartitionSpec as P

HEAD_DIM = 64
ROT = 32
epsilon = 1e-05


def layer_norm(row_data, gain_vec, bias_vec):
    values = row_data.astype(jnp.float32)
    row_mean = jnp.mean(values, axis=-1, keepdims=True)
    centered = values - row_mean
    spread = jnp.mean(centered * centered, axis=-1, keepdims=True)
    return centered * lax.rsqrt(spread + epsilon) * gain_vec + bias_vec


def rotate(head_rows, positions):
    half_rot = ROT // 2
    inverse = 10000.0 ** (-2.0 * jnp.arange(half_rot, dtype=jnp.float32) / ROT)
    angles = positions.astype(jnp.float32)[:, None] * inverse[None, :]
    cosine = jnp.cos(angles)[:, None, :]
    sine = jnp.sin(angles)[:, None, :]
    lower = head_rows[..., :half_rot]
    upper = head_rows[..., half_rot:ROT]
    return jnp.concatenate(
        [lower * cosine - upper * sine, upper * cosine + lower * sine, head_rows[..., ROT:]],
        axis=-1,
    )


def run_starts(token_request):
    tok_total = token_request.shape[0]
    token_index = jnp.arange(tok_total, dtype=jnp.int32)
    change = jnp.concatenate([jnp.ones((1,), dtype=bool), token_request[1:] != token_request[:-1]])
    return (token_index, lax.cummax(jnp.where(change, token_index, 0), axis=0))


def row_folder(left_rows, running, w_piece):
    columns_part = lax.slice_in_dim(left_rows, 0, w_piece.shape[0], axis=1)
    return running + jnp.dot(
        columns_part, w_piece.reshape(w_piece.shape[0], -1), preferred_element_type=jnp.float32
    )


def local(
    residual_in,
    mlp_branch,
    norm_gain,
    norm_bias,
    w_qkv,
    qkv_bias,
    cache_pool,
    w_dense,
    dense_bias,
    next_gain,
    next_bias,
    w_next,
    next_qkv_bias,
    token_request,
    cache_len,
    block_table,
):
    full_rows = lax.all_gather(residual_in, "mp", axis=1, tiled=True)
    tok_count = full_rows.shape[0]
    col_width = w_qkv.shape[2]
    head_count = col_width // HEAD_DIM
    normed = layer_norm(full_rows, norm_gain, norm_bias).astype(jnp.bfloat16)
    empty_sum = jnp.zeros((tok_count, 3 * col_width), jnp.float32)
    w_rows = w_qkv.shape[0]
    dense_shard = w_dense.reshape(w_rows, -1)
    joined = jnp.concatenate(
        [w_qkv.reshape(w_rows, -1), w_next.reshape(w_rows, -1), dense_shard], axis=1
    )
    gathered = lax.all_gather(joined, "pool", axis=0, tiled=True)
    qkv_cols = 3 * col_width
    w_qkv_full = gathered[:, :qkv_cols]
    w_next_full = gathered[:, qkv_cols : 2 * qkv_cols]
    pool_total = lax.axis_size("pool")
    w_dense_full = (
        gathered[:, 2 * qkv_cols :]
        .reshape((pool_total,) + w_dense.shape)
        .transpose(1, 0, 2)
        .reshape(w_dense.shape[0], -1)
    )
    projected = row_folder(normed, empty_sum, w_qkv_full)
    projected = (projected + qkv_bias.reshape(1, 3 * col_width)).reshape(tok_count, 3, col_width)
    token_index, starts = run_starts(token_request)
    request_count = cache_len.shape[0]
    local_req = token_request - request_count * lax.axis_index("pool")
    request_ids = jnp.arange(request_count, dtype=jnp.int32)
    request_match = local_req[:, None] == request_ids[None, :]
    cached_here = jnp.sum(jnp.where(request_match, cache_len[None, :], 0), axis=1)
    positions = cached_here + token_index - starts
    query = rotate(projected[:, 0].reshape(tok_count, head_count, HEAD_DIM), positions).astype(
        jnp.bfloat16
    )
    key_new = rotate(projected[:, 1].reshape(tok_count, head_count, HEAD_DIM), positions).astype(
        jnp.bfloat16
    )
    value_new = projected[:, 2].reshape(tok_count, head_count, HEAD_DIM).astype(jnp.bfloat16)
    pool_count = lax.axis_size("pool")
    blocks_here = cache_pool.shape[0]
    entries = block_table.reshape(-1)
    holder_order = jnp.argsort(entries // blocks_here, stable=True)
    slot_ids = (entries % blocks_here)[holder_order].reshape(pool_count, -1)
    wanted = lax.all_to_all(slot_ids, "pool", split_axis=0, concat_axis=0, tiled=True)
    packed = cache_pool[wanted.reshape(-1)].reshape((pool_count, -1) + cache_pool.shape[1:])
    arrived = lax.all_to_all(packed, "pool", split_axis=0, concat_axis=0, tiled=True)
    table_blocks = arrived.reshape((-1,) + cache_pool.shape[1:])[jnp.argsort(holder_order)]
    span = block_table.shape[1] * cache_pool.shape[2]
    slot_total = request_count * span
    cached_keys = table_blocks[:, 0].reshape(slot_total, head_count, HEAD_DIM)
    cached_values = table_blocks[:, 1].reshape(slot_total, head_count, HEAD_DIM)
    slot_index = jnp.arange(slot_total, dtype=jnp.int32)
    slot_req = slot_index // span
    slot_len = jnp.repeat(cache_len, span, total_repeat_length=slot_total)
    cache_ok = (slot_req[None, :] == local_req[:, None]) & (slot_index % span < slot_len)[None, :]
    new_ok = (token_request[None, :] == token_request[:, None]) & (
        token_index[None, :] <= token_index[:, None]
    )
    allowed = jnp.concatenate([cache_ok, new_ok], axis=1)
    key_all = jnp.concatenate([cached_keys, key_new], axis=0).transpose(1, 0, 2)
    value_all = jnp.concatenate([cached_values, value_new], axis=0).transpose(1, 0, 2)
    score_scale = HEAD_DIM ** (-0.5)

    def one_head(operands):
        q_head, k_head, v_head = operands
        scores = (
            jnp.einsum("qd,kd->qk", q_head, k_head, preferred_element_type=jnp.float32)
            * score_scale
        )
        scores = jnp.where(allowed, scores, -1e30)
        row_max = jnp.max(scores, axis=1, keepdims=True)
        weights = jnp.exp(scores - row_max)
        probs = (weights / jnp.sum(weights, axis=1, keepdims=True)).astype(jnp.bfloat16)
        return jnp.dot(probs, v_head, preferred_element_type=jnp.float32).astype(jnp.bfloat16)

    mixed = lax.map(one_head, (query.transpose(1, 0, 2), key_all, value_all))
    attended = mixed.transpose(1, 0, 2).reshape(tok_count, col_width)
    partial_out = jnp.dot(attended, w_dense_full, preferred_element_type=jnp.float32)
    mp_index = lax.axis_index("mp")
    dense_total = lax.psum(partial_out.astype(jnp.bfloat16), "mp").astype(jnp.float32)
    whole_hidden = (
        full_rows.astype(jnp.float32) + dense_total + dense_bias + mlp_branch.astype(jnp.float32)
    ).astype(jnp.bfloat16)
    hidden_out = lax.dynamic_slice_in_dim(whole_hidden, mp_index * col_width, col_width, 1)
    normed_next = layer_norm(whole_hidden, next_gain, next_bias).astype(jnp.bfloat16)
    next_raw = row_folder(normed_next, empty_sum, w_next_full)
    next_qkv = (
        (next_raw + next_qkv_bias.reshape(1, 3 * col_width))
        .astype(jnp.bfloat16)
        .reshape(tok_count, 3, col_width)
    )
    return (hidden_out, next_qkv)


def solution(mesh):
    in_specs = (
        P("pool", "mp"),
        P("pool", None),
        P(),
        P(),
        P("pool", None, "mp"),
        P(None, "mp"),
        P("pool", None, None, "mp"),
        P("mp", "pool"),
        P(),
        P(),
        P(),
        P("pool", None, "mp"),
        P(None, "mp"),
        P("pool"),
        P("pool"),
        P("pool", None),
    )
    out_specs = (P("pool", "mp"), P("pool", None, "mp"))
    return jax.shard_map(local, mesh=mesh, in_specs=in_specs, out_specs=out_specs, check_vma=False)
```

profile of v0, /device:TPU:2, one launch (start us, length us, event | category | flops | bytes accessed | tf_op | source)
XLA Modules:
  0.0 356.8 jit_solution(5560518545241421026)
XLA Ops:
  12.8 2.5 sort.34
  16.8 22.3 %all_to_all.14 = s32[64,1,2]{2,1,0:T(1,128)S(1)} all-to-all(s32[64,1,2]{2,1,0:T(1,128)S(1)} %bitcast.87), channel_id=1, replica_groups=mesh['pool'=64,'mp'=8] {'pool'}, dimensions={0} | all-to-all | bytes 1024 | tf_op jit(solution)/shard_map/all_to_all | solution.py:108
  40.5 2.8 gather_fusion.1
  43.3 6.6 %all-to-all-start.1 = ((bf16[64,2,2,32,256]{4,3,2,1,0:T(8,128)(2,1)}), bf16[64,2,2,32,256]{4,3,2,1,0:T(8,128)(2,1)}, u32[]{:S(2)}, u32[]{:S(2)}) async-start(bf16[64,2,2,32,256]{4,3,2,1,0:T(8,128)(2,1)} %bitcast.74), calls=%async_computation.1 | async-start | bytes 8388608 | tf_op jit(solution)/shard_map/all_to_all | solution.py:110
  50.6 2.6 sort.35
  54.2 2.6 fusion.63
  59.3 1.6 fusion.26
  61.0 97.6 %all-to-all-done.1 = bf16[64,2,2,32,256]{4,3,2,1,0:T(8,128)(2,1)} async-done(((bf16[64,2,2,32,256]{4,3,2,1,0:T(8,128)(2,1)}), bf16[64,2,2,32,256]{4,3,2,1,0:T(8,128)(2,1)}, u32[]{:S(2)}, u32[]{:S(2)}) %all-to-all-start.1) | async-done | bytes 4194336 | tf_op jit(solution)/shard_map/all_to_all | solution.py:110
  158.6 5.0 %gather_fusion.2 = bf16[128,2,32,256]{3,2,1,0:T(8,128)(2,1)} fusion(bf16[128,2,32,256]{3,2,1,0:T(8,128)(2,1)} %bitcast.12, s32[1024]{0:T(1024)S(1)} %pad_clamp_fusion), kind=kCustom, calls=%fused_computation.2 | custom fusion | bytes 8389120 | tf_op jit(solution)/shard_map/gather | solution.py:111
  163.6 4.8 %fusion.70 = (bf16[128,1,32,256]{3,2,1,0:T(8,128)(2,1)}, bf16[128,1,32,256]{3,2,1,0:T(8,128)(2,1)}) fusion(bf16[128,2,32,256]{3,2,1,0:T(8,128)(2,1)} %gather_fusion.2), kind=kLoop, calls=%fused_computation.114 | loop fusion | bytes 8388608 | tf_op jit(solution)/shard_map/slice | solution.py:115
  168.3 7.1 %reshape_squeeze.14 = bf16[4096,4,64]{2,1,0:T(4,128)(2,1)} reshape(bf16[128,1,32,256]{3,2,1,0:T(8,128)(2,1)} %get-tuple-element.110) | data formatting | bytes 4194304 | tf_op jit(solution)/shard_map/reshape;squeeze | solution.py:114
  175.4 7.2 %reshape_squeeze.16 = bf16[4096,4,64]{2,1,0:T(4,128)(2,1)} reshape(bf16[128,1,32,256]{3,2,1,0:T(8,128)(2,1)} %get-tuple-element.109) | data formatting | bytes 4194304 | tf_op jit(solution)/shard_map/reshape;squeeze | solution.py:115
  182.6 3.9 %fusion.37 = f32[256,768]{1,0:T(8,128)} fusion(bf16[2048,1792]{1,0:T(8,128)(2,1)} %all-gather.5.cloned.1.call-done, bf16[256,2048]{1,0:T(8,128)(2,1)S(1)} %copy-done.2, f32[2048]{0:T(1024)S(1)} %copy-done.13, f32[2048]{0:T(1024)S(1)} %copy-done.14, f32[256]{0:T(256)S(1)} %add_rsqrt_fusion.1, f32[256]{0:T(256)S(1)} %broadcast_multiply_fusion.1, ...), kind=kOutput, calls=%fused_computation.49 | convolution fusion | flops 808648704 | bytes 5002240 | tf_op jit(solution)/shard_map/dot_general | solution.py:42
  188.2 17.7 %maximum_bitcast_fusion = bf16[4,4352,64]{2,0,1:T(4,128)(2,1)S(1)} fusion(bf16[256,4,64]{2,1,0:T(4,128)(2,1)S(1)} %copy.82, bf16[4096,4,64]{2,1,0:T(4,128)(2,1)} %reshape_squeeze.14), kind=kLoop, calls=%fused_computation.20 | loop fusion | flops 1114112 | bytes 4456448 | tf_op jit(solution)/shard_map/transpose | solution.py:124
  205.9 2.7 copy.85
  208.8 17.9 %maximum_bitcast_fusion.1 = bf16[4,4352,64]{2,0,1:T(4,128)(2,1)S(1)} fusion(bf16[256,4,64]{2,1,0:T(4,128)(2,1)S(1)} %copy.83, bf16[4096,4,64]{2,1,0:T(4,128)(2,1)} %reshape_squeeze.16), kind=kLoop, calls=%fused_computation.21 | loop fusion | flops 1114112 | bytes 4456448 | tf_op jit(solution)/shard_map/transpose | solution.py:125
  226.7 2.6 copy.86
  229.4 21.9 %while.11 = (s32[]{:T(128)}, bf16[4,256,64]{1,2,0:T(8,128)(2,1)S(1)}, bf16[4,256,64]{1,2,0:T(8,128)(2,1)S(1)}, bf16[4,4352,64]{2,1,0:T(8,128)(2,1)}, pred[256,43...) while((s32[]{:T(128)}, bf16[4,256,64]{1,2,0:T(8,128)(2,1)S(1)}, ...), condition=%wide.region_10.11_spmd, body=%wide.region_7.10_spmd.sunk | while | flops 294141440 | bytes 16784460 | solution.py:140
  229.4 2.3 fusion.80
  232.4 2.4 fusion.82
  234.8 2.3 fusion.80
  237.9 2.4 fusion.82
  240.3 2.3 fusion.80
  243.4 2.4 fusion.82
  245.8 2.3 fusion.80
  248.9 2.4 fusion.82
  252.5 3.4 reshape.322
  255.9 3.5 copy.87
  261.0 80.4 %all-reduce.2.cloned.1.call-done = bf16[256,2048]{1,0:T(8,128)(2,1)} async-done(((bf16[256,2048]{1,0:T(8,128)(2,1)}), bf16[256,2048]{1,0:T(8,128)(2,1)}) %all-reduce.2.cloned.1.call-update) | async-done | bytes 1048592 | tf_op jit(solution)/shard_map/psum | solution.py:144
  341.4 2.2 convert_reduce_fusion.1
  344.6 3.0 fusion.43
  348.7 1.6 constant_dynamic-slice_fusion
  (108 shorter events, 22.4 us)
Async XLA Ops:
  7.2 33.3 %copy-start = (bf16[48,2,32,256]{3,2,1,0:T(8,128)(2,1)S(1)}, bf16[48,2,32,256]{3,2,1,0:T(8,128)(2,1)}, u32[]{:S(2)}) copy-start(bf16[48,2,32,256]{3,2,1,0:T(8,128)(2,1)} %param.26) | copy-start | bytes 4718596
  7.2 50.7 %all-gather.3.cloned.1.call-start = ((), (), s32[]{:S(2)}) async-start(), calls=%async_computation.2 | async-start | bytes 1179648 | tf_op jit(solution)/shard_map/all_gather | solution.py:65
  7.9 174.6 %all-gather.5.cloned.1.call-start = ((), (), s32[]{:S(2)}) async-start(), calls=%async_computation.3 | async-start | bytes 7454720 | tf_op jit(solution)/shard_map/all_gather | solution.py:76
  43.2 6.7 %copy-start.8 = (f32[3,256]{1,0:T(4,128)S(1)}, f32[3,256]{1,0:T(4,128)}, u32[]{:S(2)}) copy-start(f32[3,256]{1,0:T(4,128)} %param.25) | copy-start | bytes 9220
  43.2 6.8 %copy-start.5 = (s32[256]{0:T(256)S(1)}, s32[256]{0:T(256)}, u32[]{:S(2)}) copy-start(s32[256]{0:T(256)} %param.33) | copy-start | bytes 3076
  43.2 10.1 %copy-start.6 = (s32[4]{0:T(128)S(1)}, s32[4]{0:T(128)}, u32[]{:S(2)}) copy-start(s32[4]{0:T(128)} %param.34) | copy-start | bytes 52
  43.2 11.0 %copy-start.10 = (pred[4096]{0:T(1024)(128)(4,1)S(1)}, pred[4096]{0:T(1024)(128)(4,1)}, u32[]{:S(2)}) copy-start(pred[4096]{0:T(1024)(128)(4,1)} %constant.223) | copy-start | bytes 12292
  43.2 11.0 %copy-start.11 = (pred[4096]{0:T(1024)(128)(4,1)S(1)}, pred[4096]{0:T(1024)(128)(4,1)}, u32[]{:S(2)}) copy-start(pred[4096]{0:T(1024)(128)(4,1)} %constant.224) | copy-start | bytes 12292
  43.2 10.9 %copy-start.12 = (pred[4096]{0:T(1024)(128)(4,1)S(1)}, pred[4096]{0:T(1024)(128)(4,1)}, u32[]{:S(2)}) copy-start(pred[4096]{0:T(1024)(128)(4,1)} %constant.225) | copy-start | bytes 12292
  43.3 115.3 %all-to-all-start.1 = ((bf16[64,2,2,32,256]{4,3,2,1,0:T(8,128)(2,1)}), bf16[64,2,2,32,256]{4,3,2,1,0:T(8,128)(2,1)}, u32[]{:S(2)}, u32[]{:S(2)}) async-start(bf16[64,2,2,32,256]{4,3,2,1,0:T(8,128)(2,1)} %bitcast.74), calls=%async_computation.1 | async-start | bytes 8388608 | tf_op jit(solution)/shard_map/all_to_all | solution.py:110
  49.9 291.5 %all-reduce.2.cloned.1.call-start = ((), (), s32[]{:S(2)}) async-start(), calls=%async_computation.4 | async-start | bytes 2097152 | tf_op jit(solution)/shard_map/psum | solution.py:144
  175.4 7.2 %copy-start.2 = (bf16[256,2048]{1,0:T(8,128)(2,1)S(1)}, bf16[256,2048]{1,0:T(8,128)(2,1)}, u32[]{:S(2)}) copy-start(bf16[256,2048]{1,0:T(8,128)(2,1)} %all-gather.3.cloned.1.call-done) | copy-start | bytes 3145732
  175.4 7.2 %copy-start.13 = (f32[2048]{0:T(1024)S(1)}, f32[2048]{0:T(1024)}, u32[]{:S(2)}) copy-start(f32[2048]{0:T(1024)} %param.23) | copy-start | bytes 24580
  175.4 7.2 %copy-start.14 = (f32[2048]{0:T(1024)S(1)}, f32[2048]{0:T(1024)}, u32[]{:S(2)}) copy-start(f32[2048]{0:T(1024)} %param.22) | copy-start | bytes 24580
  226.7 2.7 copy-start.4
  255.9 5.1 %copy-start.9 = (f32[3,256]{1,0:T(4,128)S(1)}, f32[3,256]{1,0:T(4,128)}, u32[]{:S(2)}) copy-start(f32[3,256]{1,0:T(4,128)} %param.32) | copy-start | bytes 9220
  255.9 85.5 %copy-start.7 = (f32[2048]{0:T(1024)S(1)}, f32[2048]{0:T(1024)}, u32[]{:S(2)}) copy-start(f32[2048]{0:T(1024)} %param.28) | copy-start | bytes 24580
  261.0 83.6 %copy-start.15 = (f32[2048]{0:T(1024)S(1)}, f32[2048]{0:T(1024)}, u32[]{:S(2)}) copy-start(f32[2048]{0:T(1024)} %param.30) | copy-start | bytes 24580
  261.0 83.6 %copy-start.16 = (f32[2048]{0:T(1024)S(1)}, f32[2048]{0:T(1024)}, u32[]{:S(2)}) copy-start(f32[2048]{0:T(1024)} %param.29) | copy-start | bytes 24580
  343.6 1.0 copy-start.3
  344.0 6.3 %copy-start.1 = (bf16[48,2,32,256]{3,2,1,0:T(8,128)(2,1)S(1)}, bf16[48,2,32,256]{3,2,1,0:T(8,128)(2,1)}, u32[]{:S(2)}) copy-start(bf16[48,2,32,256]{3,2,1,0:T(8,128)(2,1)} %param.26) | copy-start | bytes 4718596
Sparse Core Ops, SparseCore 0:
  10.0 46.8 all-gather.2
  60.8 109.1 all-gather.4
  261.1 80.2 all-reduce.1
where the time goes:
time: 358 us; the launch traced here: 357 us
  waiting for transfers between devices  179 us (50%)
  other arithmetic  56.6 us (16%)
  local copies, waits for them, and re-layouts  51 us (14%)
  matrix products  27.3 us (8%)
  blocking collectives  22.3 us (6%)
  between operations  14.1 us (4%)
  starting transfers between devices  6.75 us (2%)
    all_to_all x1, waiting for transfers between devices, local(): lax.all_to_all(packed, 'pool', split_axis=0, concat_axis=0, tiled=True)  97.6 us
    psum x1, waiting for transfers between devices, local(): lax.psum(partial_out.astype(jnp.bfloat16), 'mp').astype(jnp.float32)  80.4 us
    all_to_all x1, blocking collectives, local(): lax.all_to_all(slot_ids, 'pool', split_axis=0, concat_axis=0, tiled=True)  22.3 us
    transpose x1, other arithmetic, local(): jnp.concatenate([cached_values, value_new], axis=0).transpose(1, 0, 2)  17.9 us
    transpose x1, other arithmetic, local(): key_all = jnp.concatenate([cached_keys, key_new], axis=0).transpose(1, 0, 2)  17.7 us
    dot_general x4, matrix products, one_head(): jnp.dot(probs, v_head, preferred_element_type=jnp.float32)  9.41 us
    dot_general x4, matrix products, one_head(): jnp.einsum('qd,kd->qk', q_head, k_head, preferred_element_type=jnp.float32)  9.37 us
  transfers between devices with their start and end apart: 4, of which 2 were waited for; matrix products, arithmetic and copies ran while one was open for 13% of the time, Pallas kernels for 0%

commit v1 on v0

--- a/solution.py
+++ b/solution.py
@@ -141,7 +141,9 @@
     attended = mixed.transpose(1, 0, 2).reshape(tok_count, col_width)
     partial_out = jnp.dot(attended, w_dense_full, preferred_element_type=jnp.float32)
     mp_index = lax.axis_index("mp")
-    dense_total = lax.psum(partial_out.astype(jnp.bfloat16), "mp").astype(jnp.float32)
+    dense_total = (
+        lax.all_gather(partial_out.astype(jnp.bfloat16), "mp").sum(axis=0).astype(jnp.float32)
+    )
     whole_hidden = (
         full_rows.astype(jnp.float32) + dense_total + dense_bias + mlp_branch.astype(jnp.float32)
     ).astype(jnp.bfloat16)

time: 358 us -> 379 us (1.059)
  the two profiles are of different devices: /device:TPU:2 before, /device:TPU:1 now
where the time goes in v1:
time: 379 us; the launch traced here: 378 us
  waiting for transfers between devices  194 us (51%)
  other arithmetic  61.5 us (16%)
  local copies, waits for them, and re-layouts  51 us (13%)
  matrix products  27.2 us (7%)
  blocking collectives  23.9 us (6%)
  between operations  14.2 us (4%)
  starting transfers between devices  5.96 us (2%)
    all_to_all x1, waiting for transfers between devices, local(): lax.all_to_all(packed, 'pool', split_axis=0, concat_axis=0, tiled=True)  99.8 us
    all_gather x1, waiting for transfers between devices, local(): lax.all_gather(partial_out.astype(jnp.bfloat16), 'mp').sum(axis=0)  93.6 us
    all_to_all x1, blocking collectives, local(): lax.all_to_all(slot_ids, 'pool', split_axis=0, concat_axis=0, tiled=True)  23.9 us
    transpose x1, other arithmetic, local(): jnp.concatenate([cached_values, value_new], axis=0).transpose(1, 0, 2)  17.9 us
    transpose x1, other arithmetic, local(): key_all = jnp.concatenate([cached_keys, key_new], axis=0).transpose(1, 0, 2)  17.7 us
    dot_general x4, matrix products, one_head(): jnp.dot(probs, v_head, preferred_element_type=jnp.float32)  9.41 us
    dot_general x4, matrix products, one_head(): jnp.einsum('qd,kd->qk', q_head, k_head, preferred_element_type=jnp.float32)  9.37 us
  transfers between devices with their start and end apart: 4, of which 2 were waited for; matrix products, arithmetic and copies ran while one was open for 13% of the time, Pallas kernels for 0%

profile of v1, /device:TPU:1, one launch (start us, length us, event | category | flops | bytes accessed | tf_op | source)
XLA Modules:
  0.0 377.9 jit_solution(17704826116964292634)
XLA Ops:
  12.8 2.5 sort.34
  16.8 23.9 %all_to_all.14 = s32[64,1,2]{2,1,0:T(1,128)S(1)} all-to-all(s32[64,1,2]{2,1,0:T(1,128)S(1)} %bitcast.89), channel_id=1, replica_groups=mesh['pool'=64,'mp'=8] {'pool'}, dimensions={0} | all-to-all | bytes 1024 | tf_op jit(solution)/shard_map/all_to_all | solution.py:108
  42.1 2.8 gather_fusion.1
  44.9 5.8 %all-to-all-start.1 = ((bf16[64,2,2,32,256]{4,3,2,1,0:T(8,128)(2,1)}), bf16[64,2,2,32,256]{4,3,2,1,0:T(8,128)(2,1)}, u32[]{:S(2)}, u32[]{:S(2)}) async-start(bf16[64,2,2,32,256]{4,3,2,1,0:T(8,128)(2,1)} %bitcast.75), calls=%async_computation.1 | async-start | bytes 8388608 | tf_op jit(solution)/shard_map/all_to_all | solution.py:110
  51.4 2.6 sort.35
  55.1 2.6 fusion.63
  60.2 1.6 fusion.26
  61.9 99.8 %all-to-all-done.1 = bf16[64,2,2,32,256]{4,3,2,1,0:T(8,128)(2,1)} async-done(((bf16[64,2,2,32,256]{4,3,2,1,0:T(8,128)(2,1)}), bf16[64,2,2,32,256]{4,3,2,1,0:T(8,128)(2,1)}, u32[]{:S(2)}, u32[]{:S(2)}) %all-to-all-start.1) | async-done | bytes 4194336 | tf_op jit(solution)/shard_map/all_to_all | solution.py:110
  161.6 5.0 %gather_fusion.2 = bf16[128,2,32,256]{3,2,1,0:T(8,128)(2,1)} fusion(bf16[128,2,32,256]{3,2,1,0:T(8,128)(2,1)} %bitcast.12, s32[1024]{0:T(1024)S(1)} %pad_clamp_fusion), kind=kCustom, calls=%fused_computation.2 | custom fusion | bytes 8389120 | tf_op jit(solution)/shard_map/gather | solution.py:111
  166.6 4.7 %fusion.70 = (bf16[128,1,32,256]{3,2,1,0:T(8,128)(2,1)}, bf16[128,1,32,256]{3,2,1,0:T(8,128)(2,1)}) fusion(bf16[128,2,32,256]{3,2,1,0:T(8,128)(2,1)} %gather_fusion.2), kind=kLoop, calls=%fused_computation.114 | loop fusion | bytes 8388608 | tf_op jit(solution)/shard_map/slice | solution.py:115
  171.3 7.1 %reshape_squeeze.14 = bf16[4096,4,64]{2,1,0:T(4,128)(2,1)} reshape(bf16[128,1,32,256]{3,2,1,0:T(8,128)(2,1)} %get-tuple-element.110) | data formatting | bytes 4194304 | tf_op jit(solution)/shard_map/reshape;squeeze | solution.py:114
  178.4 7.2 %reshape_squeeze.16 = bf16[4096,4,64]{2,1,0:T(4,128)(2,1)} reshape(bf16[128,1,32,256]{3,2,1,0:T(8,128)(2,1)} %get-tuple-element.109) | data formatting | bytes 4194304 | tf_op jit(solution)/shard_map/reshape;squeeze | solution.py:115
  185.6 3.9 %fusion.37 = f32[256,768]{1,0:T(8,128)} fusion(bf16[2048,1792]{1,0:T(8,128)(2,1)} %all-gather.7.cloned.1.call-done, bf16[256,2048]{1,0:T(8,128)(2,1)S(1)} %copy-done.2, f32[2048]{0:T(1024)S(1)} %copy-done.13, f32[2048]{0:T(1024)S(1)} %copy-done.14, f32[256]{0:T(256)S(1)} %add_rsqrt_fusion.1, f32[256]{0:T(256)S(1)} %broadcast_multiply_fusion.1, ...), kind=kOutput, calls=%fused_computation.49 | convolution fusion | flops 808648704 | bytes 5002240 | tf_op jit(solution)/shard_map/dot_general | solution.py:42
  191.3 17.7 %maximum_bitcast_fusion = bf16[4,4352,64]{2,0,1:T(4,128)(2,1)S(1)} fusion(bf16[256,4,64]{2,1,0:T(4,128)(2,1)S(1)} %copy.82, bf16[4096,4,64]{2,1,0:T(4,128)(2,1)} %reshape_squeeze.14), kind=kLoop, calls=%fused_computation.20 | loop fusion | flops 1114112 | bytes 4456448 | tf_op jit(solution)/shard_map/transpose | solution.py:124
  208.9 2.7 copy.85
  211.8 17.9 %maximum_bitcast_fusion.1 = bf16[4,4352,64]{2,0,1:T(4,128)(2,1)S(1)} fusion(bf16[256,4,64]{2,1,0:T(4,128)(2,1)S(1)} %copy.83, bf16[4096,4,64]{2,1,0:T(4,128)(2,1)} %reshape_squeeze.16), kind=kLoop, calls=%fused_computation.21 | loop fusion | flops 1114112 | bytes 4456448 | tf_op jit(solution)/shard_map/transpose | solution.py:125
  229.7 2.6 copy.86
  232.4 21.9 %while.11 = (s32[]{:T(128)}, bf16[4,256,64]{1,2,0:T(8,128)(2,1)S(1)}, bf16[4,256,64]{1,2,0:T(8,128)(2,1)S(1)}, bf16[4,4352,64]{2,1,0:T(8,128)(2,1)}, pred[256,43...) while((s32[]{:T(128)}, bf16[4,256,64]{1,2,0:T(8,128)(2,1)S(1)}, ...), condition=%wide.region_10.11_spmd, body=%wide.region_7.10_spmd.sunk | while | flops 294141440 | bytes 16784460 | solution.py:140
  232.4 2.3 fusion.80
  235.5 2.4 fusion.82
  237.8 2.3 fusion.80
  240.9 2.4 fusion.82
  243.3 2.3 fusion.80
  246.4 2.4 fusion.82
  248.8 2.3 fusion.80
  251.9 2.4 fusion.82
  255.5 3.4 reshape.322
  258.9 3.5 copy.87
  264.0 93.6 %all-gather.9.cloned.1.call-done = bf16[2048,2048]{1,0:T(8,128)(2,1)} async-done(((bf16[256,2048]{1,0:T(8,128)(2,1)}), bf16[2048,2048]{1,0:T(8,128)(2,1)}) %all-gather.9.cloned.1.call-update) | async-done | bytes 8388624 | tf_op jit(solution)/shard_map/all_gather | solution.py:145
  357.6 5.2 %reduce_sum.69 = bf16[256,2048]{1,0:T(8,128)(2,1)S(1)} reduce(bf16[8,256,2048]{2,1,0:T(8,128)(2,1)} %bitcast.76, bf16[]{:T(256)} %constant.191.clone.1), dimensions={0}, to_apply=%region_11.12 | reduce | flops 3670016 | bytes 9437186 | tf_op jit(solution)/shard_map/reduce_sum | solution.py:145
  362.8 1.9 convert_reduce_fusion.1
  365.7 3.0 fusion.43
  (109 shorter events, 23.9 us)
Async XLA Ops:
  7.2 34.9 %copy-start = (bf16[48,2,32,256]{3,2,1,0:T(8,128)(2,1)S(1)}, bf16[48,2,32,256]{3,2,1,0:T(8,128)(2,1)}, u32[]{:S(2)}) copy-start(bf16[48,2,32,256]{3,2,1,0:T(8,128)(2,1)} %param.26) | copy-start | bytes 4718596
  7.2 51.6 %all-gather.5.cloned.1.call-start = ((), (), s32[]{:S(2)}) async-start(), calls=%async_computation.2 | async-start | bytes 1179648 | tf_op jit(solution)/shard_map/all_gather | solution.py:65
  7.9 177.7 %all-gather.7.cloned.1.call-start = ((), (), s32[]{:S(2)}) async-start(), calls=%async_computation.3 | async-start | bytes 7454720 | tf_op jit(solution)/shard_map/all_gather | solution.py:76
  44.9 6.0 %copy-start.8 = (f32[3,256]{1,0:T(4,128)S(1)}, f32[3,256]{1,0:T(4,128)}, u32[]{:S(2)}) copy-start(f32[3,256]{1,0:T(4,128)} %param.25) | copy-start | bytes 9220
  44.9 6.0 %copy-start.5 = (s32[256]{0:T(256)S(1)}, s32[256]{0:T(256)}, u32[]{:S(2)}) copy-start(s32[256]{0:T(256)} %param.33) | copy-start | bytes 3076
  44.9 9.3 %copy-start.6 = (s32[4]{0:T(128)S(1)}, s32[4]{0:T(128)}, u32[]{:S(2)}) copy-start(s32[4]{0:T(128)} %param.34) | copy-start | bytes 52
  44.9 10.2 %copy-start.10 = (pred[4096]{0:T(1024)(128)(4,1)S(1)}, pred[4096]{0:T(1024)(128)(4,1)}, u32[]{:S(2)}) copy-start(pred[4096]{0:T(1024)(128)(4,1)} %constant.224) | copy-start | bytes 12292
  44.9 10.2 %copy-start.11 = (pred[4096]{0:T(1024)(128)(4,1)S(1)}, pred[4096]{0:T(1024)(128)(4,1)}, u32[]{:S(2)}) copy-start(pred[4096]{0:T(1024)(128)(4,1)} %constant.225) | copy-start | bytes 12292
  44.9 10.2 %copy-start.12 = (pred[4096]{0:T(1024)(128)(4,1)S(1)}, pred[4096]{0:T(1024)(128)(4,1)}, u32[]{:S(2)}) copy-start(pred[4096]{0:T(1024)(128)(4,1)} %constant.226) | copy-start | bytes 12292
  44.9 116.7 %all-to-all-start.1 = ((bf16[64,2,2,32,256]{4,3,2,1,0:T(8,128)(2,1)}), bf16[64,2,2,32,256]{4,3,2,1,0:T(8,128)(2,1)}, u32[]{:S(2)}, u32[]{:S(2)}) async-start(bf16[64,2,2,32,256]{4,3,2,1,0:T(8,128)(2,1)} %bitcast.75), calls=%async_computation.1 | async-start | bytes 8388608 | tf_op jit(solution)/shard_map/all_to_all | solution.py:110
  50.8 306.8 %all-gather.9.cloned.1.call-start = ((), (), s32[]{:S(2)}) async-start(), calls=%async_computation.4 | async-start | bytes 9437184 | tf_op jit(solution)/shard_map/all_gather | solution.py:145
  178.4 7.2 %copy-start.2 = (bf16[256,2048]{1,0:T(8,128)(2,1)S(1)}, bf16[256,2048]{1,0:T(8,128)(2,1)}, u32[]{:S(2)}) copy-start(bf16[256,2048]{1,0:T(8,128)(2,1)} %all-gather.5.cloned.1.call-done) | copy-start | bytes 3145732
  178.4 7.2 %copy-start.13 = (f32[2048]{0:T(1024)S(1)}, f32[2048]{0:T(1024)}, u32[]{:S(2)}) copy-start(f32[2048]{0:T(1024)} %param.23) | copy-start | bytes 24580
  178.4 7.2 %copy-start.14 = (f32[2048]{0:T(1024)S(1)}, f32[2048]{0:T(1024)}, u32[]{:S(2)}) copy-start(f32[2048]{0:T(1024)} %param.22) | copy-start | bytes 24580
  229.7 2.7 copy-start.4
  258.9 5.0 %copy-start.9 = (f32[3,256]{1,0:T(4,128)S(1)}, f32[3,256]{1,0:T(4,128)}, u32[]{:S(2)}) copy-start(f32[3,256]{1,0:T(4,128)} %param.32) | copy-start | bytes 9220
  357.6 5.2 %copy-start.7 = (f32[2048]{0:T(1024)S(1)}, f32[2048]{0:T(1024)}, u32[]{:S(2)}) copy-start(f32[2048]{0:T(1024)} %param.28) | copy-start | bytes 24580
  362.8 2.9 copy-start.15
  362.8 2.9 copy-start.16
  364.7 1.0 copy-start.3
  365.1 6.3 %copy-start.1 = (bf16[48,2,32,256]{3,2,1,0:T(8,128)(2,1)S(1)}, bf16[48,2,32,256]{3,2,1,0:T(8,128)(2,1)}, u32[]{:S(2)}) copy-start(bf16[48,2,32,256]{3,2,1,0:T(8,128)(2,1)} %param.26) | copy-start | bytes 4718596
Sparse Core Ops, SparseCore 0:
  10.0 43.6 all-gather.4
  57.6 113.7 all-gather.6
  264.1 93.4 all-gather.8
